TPU v7x, 32 devices: a whole 2x2x4 slice. The times are simulated.
32 devices in a mesh: ctx: 8 (over y, x, core), tp: 4 (over z).
Axes of the slice: x: 2, y: 2, z: 4, core: 2. Of those that a mesh axis runs over, the one named last changes fastest.
Arguments:
- tokens: bfloat16 [4096, 4096], P(('ctx', 'tp')), may hold values from -6 to 6
- spike_query: int32 [4096, 32], P('ctx', 'tp'), may hold values 0 or 1
- spike_key: int32 [4096, 32], P('ctx', 'tp'), may hold values 0 or 1
- qkv_weight: bfloat16 [4096, 3, 4096], P(None, None, 'tp'), may hold values from -0.09375 to 0.09375
- qkv_blocks: int32 [3, 32, 32], P(None, None, 'tp'), may hold values 0 or 1
- out_weight: bfloat16 [4096, 4096], P('tp'), may hold values from -0.09375 to 0.09375
- out_blocks: int32 [32, 32], P('tp'), may hold values 0 or 1
- cotangent: bfloat16 [4096, 4096], P(('ctx', 'tp')), may hold values from -6 to 6
Outputs:
- layer_out: bfloat16 [4096, 4096], P(('ctx', 'tp'))
- token_grad: bfloat16 [4096, 4096], P(('ctx', 'tp'))
- qkv_grad: float32 [4096, 3, 4096], P('ctx', None, 'tp')
- out_grad: float32 [4096, 4096], P('tp', 'ctx')
All inputs are finite; a program needn't handle non-finite values. No bound on the sum of `spike_query` or of `spike_key` or of `qkv_blocks` or of `out_blocks` on one device may be relied on, other than what follows from the above.
Results may differ from a plain program's by a relative error of at most 0.014.
Values may be sent and summed in bfloat16 or wider, within the bound.
No kernel may reach another device: no remote copies, remote signals or barrier semaphores. Data moves between devices by JAX's collectives and lax.ppermute only.
A program may use at most 320 MiB of HBM per device.

v0:
```python
import math
import jax
import jax.numpy as jnp
from jax import lax
from jax.sharding import PartitionSpec as P

BLOCK = 128
EPSILON = 1e-05


def carried_in(value, axis, join, neutral):
    place = lax.axis_index(axis)
    gathered = lax.all_gather(value.astype(jnp.bfloat16), axis)
    state = jnp.zeros_like(value) + jnp.asarray(neutral, value.dtype)

    def carried_one(lap, state):
        return join(state, lax.dynamic_index_in_dim(gathered, lap, 0, False).astype(value.dtype))

    return lax.fori_loop(0, place, carried_one, state)


def entering(value, axis, join, neutral):
    count = lax.axis_size(axis)
    place = lax.axis_index(axis)
    ahead = count - 1 - place
    gathered = lax.all_gather(
        value.astype(jnp.bfloat16 if value.dtype == jnp.float32 else value.dtype), axis
    )
    state = jnp.zeros_like(value) + jnp.asarray(neutral, value.dtype)

    def entering_one(lap, state):
        source = count - 1 - lap
        return join(state, lax.dynamic_index_in_dim(gathered, source, 0, False).astype(value.dtype))

    return lax.fori_loop(0, ahead, entering_one, state)


def expand_blocks(blocks):
    row_blocks, col_blocks = blocks.shape
    spread = jnp.broadcast_to(
        blocks.astype(jnp.bfloat16)[:, None, :, None], (row_blocks, BLOCK, col_blocks, BLOCK)
    )
    return spread.reshape(row_blocks * BLOCK, col_blocks * BLOCK)


def qkv_keep_table(qkv_blocks):
    tables = [expand_blocks(qkv_blocks[projection]) for projection in range(3)]
    return jnp.stack(tables, axis=1)


def add_states(earlier, following):
    return earlier + following


def on_device(
    tokens, spike_query, spike_key, qkv_weight, qkv_blocks, out_weight, out_blocks, cotangent
):
    model_width = tokens.shape[1]
    block_rows = spike_query.shape[0]
    local_heads = spike_query.shape[1]
    features = qkv_weight.shape[2]
    head_width = features // local_heads
    highest = lax.Precision.HIGHEST
    qkv_keep = qkv_keep_table(qkv_blocks).reshape(model_width, 3 * features)
    qkv_used = qkv_weight.reshape(model_width, 3 * features) * qkv_keep
    out_used = out_weight * expand_blocks(out_blocks)
    gathered = lax.all_gather(tokens, "tp", axis=0, tiled=True)
    projected = jnp.dot(gathered, qkv_used, preferred_element_type=jnp.float32).astype(jnp.bfloat16)
    projected = projected.reshape(block_rows, 3, local_heads, head_width)
    query_spikes = spike_query.astype(jnp.bfloat16)[:, :, None]
    key_spikes = spike_key.astype(jnp.bfloat16)[:, :, None]
    query_spiked = projected[:, 0] * query_spikes
    key_spiked = projected[:, 1] * key_spikes
    values = projected[:, 2]
    query_wide = query_spiked.astype(jnp.float32)
    key_wide = key_spiked.astype(jnp.float32)
    local_state = jnp.einsum("shd,she->hde", key_spiked, values, preferred_element_type=jnp.float32)
    zeros_state = jnp.zeros_like(local_state)
    prior_state = carried_in(local_state, "ctx", add_states, zeros_state)
    positions = lax.iota(jnp.int32, block_rows)
    causal_keep = positions[:, None] >= positions[None, :]
    scores = jnp.einsum(
        "thd,shd->hts", query_spiked, key_spiked, preferred_element_type=jnp.float32
    )
    scores = jnp.where(causal_keep, scores, 0.0).astype(jnp.bfloat16)
    mixed_rows = jnp.einsum("hts,she->the", scores, values, preferred_element_type=jnp.float32)
    mixed_rows = mixed_rows + jnp.einsum("thd,hde->the", query_wide, prior_state, precision=highest)
    inv_rms = lax.rsqrt(jnp.mean(mixed_rows * mixed_rows, axis=-1, keepdims=True) + EPSILON)
    normed = mixed_rows * inv_rms
    attended = normed.astype(jnp.bfloat16).reshape(block_rows, features)
    row_piece = attended
    head_sum = lax.psum_scatter(
        jnp.dot(row_piece, out_used, preferred_element_type=jnp.float32).astype(jnp.bfloat16),
        "tp",
        scatter_dimension=0,
        tiled=True,
    ).astype(jnp.float32)
    layer_out = (tokens.astype(jnp.float32) + head_sum).astype(jnp.bfloat16)
    grad_rows = lax.all_gather(cotangent, "tp", axis=0, tiled=True)
    grad_attended = jnp.einsum("tm,fm->tf", grad_rows, out_used, preferred_element_type=jnp.float32)
    grad_attended = grad_attended.reshape(block_rows, local_heads, head_width)
    inner_mean = jnp.mean(grad_attended * normed, axis=-1, keepdims=True)
    grad_mixed = inv_rms * (grad_attended - normed * inner_mean)
    grad_low = grad_mixed.astype(jnp.bfloat16)
    local_adjoint = jnp.einsum("thd,the->hde", query_wide, grad_mixed, precision=highest)
    after_state = entering(local_adjoint, "ctx", add_states, zeros_state)
    adjoint_scores = jnp.einsum(
        "the,she->hts", grad_low, values, preferred_element_type=jnp.float32
    )
    adjoint_scores = jnp.where(causal_keep, adjoint_scores, 0.0).astype(jnp.bfloat16)
    grad_query = jnp.einsum(
        "hts,shd->thd", adjoint_scores, key_spiked, preferred_element_type=jnp.float32
    )
    grad_query = grad_query + jnp.einsum("the,hde->thd", grad_mixed, prior_state, precision=highest)
    grad_key = jnp.einsum(
        "hts,thd->shd", adjoint_scores, query_spiked, preferred_element_type=jnp.float32
    )
    grad_key = grad_key + jnp.einsum(
        "she,hde->shd", values.astype(jnp.float32), after_state, precision=highest
    )
    grad_value = jnp.einsum("hts,the->she", scores, grad_low, preferred_element_type=jnp.float32)
    grad_value = grad_value + jnp.einsum("shd,hde->she", key_wide, after_state, precision=highest)
    grad_proj = jnp.stack(
        [
            (grad_query * query_spikes.astype(jnp.float32)).astype(jnp.bfloat16),
            (grad_key * key_spikes.astype(jnp.float32)).astype(jnp.bfloat16),
            grad_value.astype(jnp.bfloat16),
        ],
        axis=1,
    ).reshape(block_rows, 3 * features)
    row_piece = grad_proj
    token_sum = lax.psum_scatter(
        jnp.einsum("tc,mc->tm", row_piece, qkv_used, preferred_element_type=jnp.float32).astype(
            jnp.bfloat16
        ),
        "tp",
        scatter_dimension=0,
        tiled=True,
    ).astype(jnp.float32)
    token_grad = (cotangent.astype(jnp.float32) + token_sum).astype(jnp.bfloat16)
    out_keep_cols = expand_blocks(jnp.transpose(out_blocks))
    slice_rows = model_width // lax.axis_size("ctx")
    norm_factor = 1.0 / math.sqrt(block_rows * lax.axis_size("ctx"))
    qkv_part = jnp.einsum("tm,tc->mc", gathered, grad_proj, preferred_element_type=jnp.float32)
    qkv_part = qkv_part * qkv_keep
    out_part = jnp.einsum("tm,tf->mf", grad_rows, attended, preferred_element_type=jnp.float32)
    out_part = out_part * out_keep_cols
    weight_sum = lax.psum_scatter(
        jnp.concatenate([qkv_part, out_part], axis=1).astype(jnp.bfloat16),
        "ctx",
        scatter_dimension=0,
        tiled=True,
    ).astype(jnp.float32)
    weight_sum = weight_sum * norm_factor
    qkv_grad = weight_sum[:, : 3 * features].reshape(slice_rows, 3, features)
    out_grad = jnp.transpose(weight_sum[:, 3 * features :])
    return (layer_out, token_grad, qkv_grad, out_grad)


def solution(mesh):
    placed = (
        P(("ctx", "tp"), None),
        P("ctx", "tp"),
        P("ctx", "tp"),
        P(None, None, "tp"),
        P(None, None, "tp"),
        P("tp", None),
        P("tp", None),
        P(("ctx", "tp"), None),
    )
    return jax.shard_map(
        on_device,
        mesh=mesh,
        in_specs=placed,
        out_specs=(
            P(("ctx", "tp"), None),
            P(("ctx", "tp"), None),
            P("ctx", None, "tp"),
            P("tp", "ctx"),
        ),
        check_vma=False,
    )
```

profile of v0, /device:TPU:0, one launch (start us, length us, event | category | flops | bytes accessed | tf_op | source)
XLA Modules:
  0.0 714.5 jit_solution(4649358727200529671)
XLA Ops:
  7.2 0.7 all-gather.7.cloned.1.call-update
  8.0 32.2 %copy.43 = bf16[4096,3,1024]{0,2,1:T(8,128)(2,1)} copy(bf16[4096,3,1024]{2,0,1:T(8,128)(2,1)} %param.15) | data formatting | bytes 50331648 | tf_op args[3]
  40.2 4.5 broadcast_in_dim.22
  44.7 13.3 %stack_reshape.9 = bf16[4096,1,1024]{0,2,1:T(8,128)(2,1)} reshape(bf16[32,128,8,128]{1,0,3,2:T(8,128)(2,1)} %broadcast_in_dim.22) | data formatting | bytes 16777216 | tf_op jit(solution)/shard_map/stack;reshape | solution.py:48
  58.0 4.5 broadcast_in_dim.25
  62.5 13.3 %stack_reshape.10 = bf16[4096,1,1024]{0,2,1:T(8,128)(2,1)} reshape(bf16[32,128,8,128]{1,0,3,2:T(8,128)(2,1)} %broadcast_in_dim.25) | data formatting | bytes 16777216 | tf_op jit(solution)/shard_map/stack;reshape | solution.py:48
  75.8 4.5 broadcast_in_dim.26
  80.3 13.4 %stack_reshape.11 = bf16[4096,1,1024]{0,2,1:T(8,128)(2,1)} reshape(bf16[32,128,8,128]{1,0,3,2:T(8,128)(2,1)} %broadcast_in_dim.26) | data formatting | bytes 16777216 | tf_op jit(solution)/shard_map/stack;reshape | solution.py:48
  93.7 7.8 %constant_dynamic-update-slice_fusion.2 = bf16[4096,3,1024]{0,2,1:T(8,128)(2,1)} fusion(bf16[4096,1,1024]{0,2,1:T(8,128)(2,1)} %stack_reshape.9), kind=kLoop, calls=%fused_computation.51 | loop fusion | bytes 16777216
  101.5 7.7 %constant_dynamic-update-slice_fusion.1 = bf16[4096,3,1024]{0,2,1:T(8,128)(2,1)} fusion(bf16[4096,3,1024]{0,2,1:T(8,128)(2,1)} %constant_dynamic-update-slice_fusion.2, bf16[4096,1,1024]{0,2,1:T(8,128)(2,1)} %stack_reshape.10), kind=kLoop, calls=%fused_computation.50 | loop fusion | bytes 16777216
  109.2 7.8 %constant_dynamic-update-slice_fusion = bf16[4096,3,1024]{0,2,1:T(8,128)(2,1)} fusion(bf16[4096,3,1024]{0,2,1:T(8,128)(2,1)} %constant_dynamic-update-slice_fusion.1, bf16[4096,1,1024]{0,2,1:T(8,128)(2,1)} %stack_reshape.11), kind=kLoop, calls=%fused_computation.49 | loop fusion | bytes 16777216 | tf_op jit(solution)/shard_map/stack | solution.py:48
  117.0 28.6 %mul.82 = bf16[4096,3,1024]{0,2,1:T(8,128)(2,1)} multiply(bf16[4096,3,1024]{0,2,1:T(8,128)(2,1)} %copy.43, bf16[4096,3,1024]{0,2,1:T(8,128)(2,1)} %constant_dynamic-update-slice_fusion) | non-fusion elementwise | flops 12582912 | bytes 75497472 | tf_op jit(solution)/shard_map/mul | solution.py:65
  145.7 18.2 %convolution_convert_fusion.2 = bf16[3072,512]{1,0:T(8,128)(2,1)S(1)} fusion(bf16[4096,3072]{0,1:T(8,128)(2,1)} %bitcast.148, bf16[512,4096]{1,0:T(8,128)(2,1)} %all-gather.7.cloned.1.call-done), kind=kOutput, calls=%fused_computation.13 | convolution fusion | flops 12886474752 | bytes 32505856 | tf_op jit(solution)/shard_map/dot_general | solution.py:68
  163.9 1.5 convolution_convert_fusion.3
  165.4 0.7 all-gather.9.cloned.1.call-update
  166.1 0.2 all-gather.13.cloned.1.call-start
  166.3 0.1 iota_compare_fusion
  166.5 1.4 select_convert_fusion.1
  167.9 2.0 copy-done.4
  169.9 2.8 fusion.12
  172.7 22.8 %all-gather.11.cloned.1.call-done = bf16[64,128,128]{2,1,0:T(8,128)(2,1)} async-done(((bf16[8,128,128]{2,1,0:T(8,128)(2,1)}), bf16[64,128,128]{2,1,0:T(8,128)(2,1)}) %all-gather.11.cloned.1.call-update) | async-done | bytes 2097168 | tf_op jit(solution)/shard_map/all_gather | solution.py:13
  195.5 3.1 fusion.5
  198.6 79.2 %all-gather.9.cloned.1.call-done = bf16[512,4096]{1,0:T(8,128)(2,1)} async-done(((bf16[128,4096]{1,0:T(8,128)(2,1)}), bf16[512,4096]{1,0:T(8,128)(2,1)}) %all-gather.9.cloned.1.call-update) | async-done | bytes 4194320 | tf_op jit(solution)/shard_map/all_gather | solution.py:99
  277.8 1.1 broadcast_in_dim.30
  279.0 12.4 %multiply_reduce_fusion = (f32[512,8]{0,1:T(8,128)S(1)}, f32[1024,512]{1,0:T(8,128)S(1)}) fusion(f32[8,128,512]{2,1,0:T(8,128)S(1)} %get-tuple-element.125, f32[512,8]{0,1:T(8,128)S(1)} %add_rsqrt_fusion, bf16[512,4096]{1,0:T(8,128)(2,1)} %all-gather.9.cloned.1.call-done, bf16[1024,4096]{1,0:T(8,128)(2,1)} %param.17, bf16[128,8,32,128]{3,2,1,0:T(8,128)(2,1)S(1)} %bitcast.145), kind=kOutput, calls=%fused_computation.27 | convolution fusion | flops 4300730368 | bytes 25198592 | tf_op jit(solution)/shard_map/tm,fm->tf/dot_general | solution.py:100
  291.4 3.2 subtract_multiply_fusion
  294.6 3.1 convolution_convert_fusion.4
  297.7 0.3 reduce-scatter.4.cloned.1.call-start
  298.0 13.5 %convolution_convert_fusion.1 = bf16[512,4096]{1,0:T(8,128)(2,1)} fusion(bf16[512,1024]{0,1:T(8,128)(2,1)} %bitcast.160, bf16[1024,4096]{1,0:T(8,128)(2,1)} %param.17, bf16[128,8,32,128]{3,2,1,0:T(8,128)(2,1)} %bitcast.146), kind=kOutput, calls=%fused_computation.12 | convolution fusion | flops 4301258752 | bytes 22020096 | tf_op jit(solution)/shard_map/dot_general | solution.py:93
  311.5 0.0 reduce-scatter.6.cloned.1.call-start
  311.5 2.7 select_convert_fusion
  314.3 1.5 fusion.22
  315.8 2.9 fusion.8
  318.6 2.1 fusion.17
  320.8 0.9 copy-done.5
  321.6 2.1 fusion.13
  323.7 0.6 all-gather.13.cloned.1.call-done
  324.3 8.2 %while.23 = (s32[]{:T(128)}, f32[8,128,128]{2,1,0:T(8,128)S(1)}, s32[]{:T(128)}, bf16[8,8,128,128]{3,2,1,0:T(8,128)(2,1)}, s32[]{:T(128)}, /*index=5*/s32[]{:T(128)}, s32[]{:T(128)}, s32[]{:T(128)}) while((s32[]{:T(128)}, f32[8,128,128]{2,1,0:T(8,128)S(1)}, s32[]{:T(128)}, bf16[8,8,128,128]{3,2,1,0:T(8,128)(2,1)}, s32[]{:T(128)}, ...), condition=%wide.region_6.7_spmd, body=%wide.region_5.6_spmd.sunk | while | flops 262150 | bytes 1310863 | solution.py:35
  324.4 1.2 convert_add_fusion.5
  325.6 1.1 convert_add_fusion.5
  326.7 1.1 convert_add_fusion.5
  327.8 1.1 convert_add_fusion.5
  328.9 1.1 convert_add_fusion.5
  330.0 1.1 convert_add_fusion.5
  331.1 1.1 convert_add_fusion.5
  332.6 3.5 fusion.7
  336.1 2.3 fusion.9
  338.4 0.3 pad_maximum_fusion.1
  338.7 1.6 copy-done.12
  340.4 19.9 %convolution_convert_fusion = bf16[512,4096]{1,0:T(8,128)(2,1)} fusion(bf16[512,3072]{0,1:T(8,128)(2,1)S(1)} %bitcast.162, bf16[4096,3072]{0,1:T(8,128)(2,1)} %bitcast.149), kind=kOutput, calls=%fused_computation.11 | convolution fusion | flops 12886999040 | bytes 32505856 | tf_op jit(solution)/shard_map/tc,mc->tm/dot_general | solution.py:133
  360.3 0.0 reduce-scatter.8.cloned.1.call-start
  360.3 8.0 %broadcast_in_dim.58 = f32[32,128,8,128]{1,0,3,2:T(8,128)} broadcast(f32[32,8]{0,1:T(8,128)S(1)} %get-tuple-element.113), dimensions={0,2} | broadcast | bytes 16778240 | tf_op jit(solution)/shard_map/broadcast_in_dim | solution.py:40
  368.3 15.5 %fusion.1 = bf16[4096,1024]{0,1:T(8,128)(2,1)} fusion(f32[128,8,32,128]{3,2,1,0:T(8,128)} %bitcast.143, bf16[512,1024]{0,1:T(8,128)(2,1)S(1)} %bitcast.161, bf16[512,4096]{1,0:T(8,128)(2,1)S(1)} %copy-done.6), kind=kOutput, calls=%fused_computation.6 | convolution fusion | flops 4303355904 | bytes 30408704 | tf_op jit(solution)/shard_map/tm,tf->mf/dot_general | solution.py:146
  383.8 27.2 %fusion = bf16[4096,3072]{0,1:T(8,128)(2,1)} fusion(bf16[4096,3072]{0,1:T(8,128)(2,1)} %bitcast.144, bf16[512,3072]{0,1:T(8,128)(2,1)} %bitcast.163, bf16[512,4096]{1,0:T(8,128)(2,1)} %all-gather.7.cloned.1.call-done), kind=kOutput, calls=%fused_computation.3 | convolution fusion | flops 12922650624 | bytes 57671680 | tf_op jit(solution)/shard_map/tm,tc->mc/dot_general | solution.py:144
  411.0 24.0 %pad_maximum_fusion = bf16[4096,4096]{0,1:T(8,128)(2,1)} fusion(bf16[4096,1024]{0,1:T(8,128)(2,1)} %fusion.1, bf16[4096,3072]{0,1:T(8,128)(2,1)} %fusion), kind=kLoop, calls=%fused_computation.4 | loop fusion | flops 67108864 | bytes 67108864 | tf_op jit(solution)/shard_map/concatenate | solution.py:149
  435.1 1.1 copy-done.9
  436.2 2.4 add_convert_fusion.2
  438.7 44.7 %reduce-scatter.6.cloned.1.call-done = bf16[128,4096]{1,0:T(8,128)(2,1)} async-done(((bf16[512,4096]{1,0:T(8,128)(2,1)}), bf16[128,4096]{1,0:T(8,128)(2,1)}) %reduce-scatter.6.cloned.1.call-update) | async-done | bytes 1048592 | tf_op jit(solution)/shard_map/reduce_scatter | solution.py:132
  483.4 2.4 add_convert_fusion
  485.8 206.9 %reduce-scatter.8.cloned.1.call-done = bf16[512,4096]{0,1:T(8,128)(2,1)} async-done(((bf16[4096,4096]{0,1:T(8,128)(2,1)}), bf16[512,4096]{0,1:T(8,128)(2,1)}) %reduce-scatter.8.cloned.1.call-update) | async-done | bytes 4194320 | tf_op jit(solution)/shard_map/reduce_scatter | solution.py:148
  692.7 3.4 convert_multiply_fusion.1
  696.1 3.3 slice.41
  699.4 1.5 slice_bitcast_fusion
  700.9 6.6 copy.56
  (49 shorter events, 0.4 us)
Async XLA Ops:
  7.2 138.5 %all-gather.7.cloned.1.call-start = ((), (), s32[]{:S(2)}) async-start(), calls=%async_computation.3 | async-start | bytes 5242880 | tf_op jit(solution)/shard_map/all_gather | solution.py:67
  7.9 32.3 %copy-start.15 = (s32[3,32,8]{1,2,0:T(8,128)S(1)}, s32[3,32,8]{1,2,0:T(8,128)}, u32[]{:S(2)}) copy-start(s32[3,32,8]{1,2,0:T(8,128)} %param.16) | copy-start | bytes 9220
  7.9 187.5 %all-gather.11.cloned.1.call-start = ((), (), s32[]{:S(2)}) async-start(), calls=%async_computation.8 | async-start | bytes 2359296 | tf_op jit(solution)/shard_map/all_gather | solution.py:13
  117.0 28.6 %copy-start.13 = (s32[512,8]{0,1:T(8,128)S(1)}, s32[512,8]{0,1:T(8,128)}, u32[]{:S(2)}) copy-start(s32[512,8]{0,1:T(8,128)} %param.13) | copy-start | bytes 49156
  117.0 28.6 %copy-start.14 = (s32[512,8]{0,1:T(8,128)S(1)}, s32[512,8]{0,1:T(8,128)}, u32[]{:S(2)}) copy-start(s32[512,8]{0,1:T(8,128)} %param.14) | copy-start | bytes 49156
  163.8 4.0 copy-start.1
  163.8 2.6 copy-start.16
  165.4 112.4 %all-gather.9.cloned.1.call-start = ((), (), s32[]{:S(2)}) async-start(), calls=%async_computation.5 | async-start | bytes 5242880 | tf_op jit(solution)/shard_map/all_gather | solution.py:99
  166.1 158.2 %all-gather.13.cloned.1.call-start = ((), (), s32[]{:S(2)}) async-start(), calls=%async_computation.9 | async-start | bytes 2359296 | tf_op jit(solution)/shard_map/all_gather | solution.py:26
  167.9 2.0 copy-start.4
  198.6 80.4 %copy-start.3 = (f32[8,128,512]{2,1,0:T(8,128)}, f32[8,128,512]{2,1,0:T(8,128)S(1)}, u32[]{:S(2)}) copy-start(f32[8,128,512]{2,1,0:T(8,128)S(1)} %get-tuple-element.125) | copy-start | bytes 6291460
  279.0 12.4 %copy-start = (bf16[8,128,32,128]{3,2,1,0:T(8,128)(2,1)}, bf16[8,128,32,128]{3,2,1,0:T(8,128)(2,1)S(1)}, u32[]{:S(2)}) copy-start(bf16[8,128,32,128]{3,2,1,0:T(8,128)(2,1)S(1)} %broadcast_in_dim.30) | copy-start | bytes 25165828
  297.7 137.3 %reduce-scatter.4.cloned.1.call-start = ((), (), s32[]{:S(2)}) async-start(), calls=%async_computation.4 | async-start | bytes 5242880 | tf_op jit(solution)/shard_map/reduce_scatter | solution.py:92
  311.5 171.9 %reduce-scatter.6.cloned.1.call-start = ((), (), s32[]{:S(2)}) async-start(), calls=%async_computation.6 | async-start | bytes 5242880 | tf_op jit(solution)/shard_map/reduce_scatter | solution.py:132
  311.5 2.7 copy-start.2
  318.6 3.0 copy-start.5
  324.3 11.8 %copy-start.7 = (f32[8,128,512]{2,1,0:T(8,128)S(1)}, f32[8,128,512]{2,1,0:T(8,128)}, u32[]{:S(2)}) copy-start(f32[8,128,512]{2,1,0:T(8,128)} %fusion.17) | copy-start | bytes 6291460
  332.5 5.8 copy-start.11
  338.7 1.6 copy-start.12
  360.3 332.4 %reduce-scatter.8.cloned.1.call-start = ((), (), s32[]{:S(2)}) async-start(), calls=%async_computation.7 | async-start | bytes 37748736 | tf_op jit(solution)/shard_map/reduce_scatter | solution.py:148
  360.3 8.0 %copy-start.6 = (bf16[512,4096]{1,0:T(8,128)(2,1)S(1)}, bf16[512,4096]{1,0:T(8,128)(2,1)}, u32[]{:S(2)}) copy-start(bf16[512,4096]{1,0:T(8,128)(2,1)} %all-gather.9.cloned.1.call-done) | copy-start | bytes 12582916
  360.3 8.0 %copy-start.8 = (bf16[512,8,128]{0,2,1:T(8,128)(2,1)S(1)}, bf16[512,8,128]{0,2,1:T(8,128)(2,1)}, u32[]{:S(2)}) copy-start(bf16[512,8,128]{0,2,1:T(8,128)(2,1)} %get-tuple-element.120) | copy-start | bytes 3145732
  435.0 1.2 copy-start.9
  435.0 48.4 %copy-start.10 = (bf16[128,4096]{1,0:T(8,128)(2,1)S(1)}, bf16[128,4096]{1,0:T(8,128)(2,1)}, u32[]{:S(2)}) copy-start(bf16[128,4096]{1,0:T(8,128)(2,1)} %param.19) | copy-start | bytes 3145732
Sparse Core Ops, SparseCore 0:
  9.6 83.4 all-gather.6
  165.5 29.8 all-gather.10
  197.0 80.7 all-gather.8
  297.8 26.4 all-gather.12
  327.0 76.7 reduce-scatter.3
  406.1 77.2 reduce-scatter.5
  486.9 205.7 reduce-scatter.7
where the time goes:
time: 725 us; the launch traced here: 715 us
  waiting for transfers between devices  356 us (49%)
  matrix products  136 us (19%)
  local copies, waits for them, and re-layouts  135 us (19%)
  other arithmetic  72 us (10%)
  between operations  14.7 us (2%)
    reduce_scatter x1, waiting for transfers between devices, on_device(): lax.psum_scatter(jnp.concatenate([qkv_part, out_part], axis=1).astype(jnp...  207 us
    all_gather x1, waiting for transfers between devices, on_device(): grad_rows = lax.all_gather(cotangent, 'tp', axis=0, tiled=True)  79.2 us
    unnamed x38, local copies, waits for them, and re-layouts  60 us
    another operation x4, local copies, waits for them, and re-layouts, qkv_keep_table(): return jnp.stack(tables, axis=1)  47.8 us
    reduce_scatter x1, waiting for transfers between devices, on_device(): lax.psum_scatter(jnp.einsum('tc,mc->tm', row_piece, qkv_used, preferred_e...  44.7 us
    mul x1, other arithmetic, on_device(): qkv_used = qkv_weight.reshape(model_width, 3 * features) * qkv_keep  28.6 us
    dot_general x1, matrix products, on_device(): jnp.einsum('tm,tc->mc', gathered, grad_proj, preferred_element_type=jnp.f...  27.2 us
    concatenate x1, other arithmetic, on_device(): jnp.concatenate([qkv_part, out_part], axis=1).astype(jnp.bfloat16)  24 us
  transfers between devices with their start and end apart: 7, of which 5 were waited for; matrix products, arithmetic and copies ran while one was open for 40% of the time, Pallas kernels for 0%

commit v1 on v0

--- a/solution.py
+++ b/solution.py
@@ -96,7 +96,12 @@
         tiled=True,
     ).astype(jnp.float32)
     layer_out = (tokens.astype(jnp.float32) + head_sum).astype(jnp.bfloat16)
-    grad_rows = lax.all_gather(cotangent, "tp", axis=0, tiled=True)
+    ring = [cotangent]
+    for hop in range(3):
+        ring.append(lax.ppermute(ring[-1], "tp", [(dev, (dev + 1) % 4) for dev in range(4)]))
+    grad_rows = jnp.roll(
+        jnp.concatenate(ring[::-1], axis=0), (lax.axis_index("tp") + 1) * ring[0].shape[0], axis=0
+    )
     grad_attended = jnp.einsum("tm,fm->tf", grad_rows, out_used, preferred_element_type=jnp.float32)
     grad_attended = grad_attended.reshape(block_rows, local_heads, head_width)
     inner_mean = jnp.mean(grad_attended * normed, axis=-1, keepdims=True)

time: 725 us -> 676 us (0.932)
  waiting for transfers between devices: 356 us -> 285 us
  local copies, waits for them, and re-layouts: 135 us -> 146 us
  matrix products: 136 us -> 144 us
    all_gather x1 -> x0, waiting for transfers between devices: 79.2 us -> none  [on_device(): grad_rows = lax.all_gather(cotangent, 'tp', axis=0, tiled=True)]
    ppermute x0 -> x3, waiting for transfers between devices: none -> 12.2 us  [on_device(): lax.ppermute(ring[-1], 'tp', [(dev, (dev + 1) % 4) for dev in range(4)])]
    unnamed x38 -> x53, local copies, waits for them, and re-layouts: 60 us -> 70.1 us
    all_gather x1, waiting for transfers between devices: 22.8 us -> 12.9 us  [carried_in(): gathered = lax.all_gather(value.astype(jnp.bfloat16), axis)]
    all_gather x1, waiting for transfers between devices: 0.59 us -> 9.61 us  [entering(): lax.all_gather(value.astype(jnp.bfloat16 if value.dtype == jnp.float32 el...]
  transfers between devices with their start and end apart: 7 -> 9, of which waited for: 5 -> 5; matrix products, arithmetic and copies ran while one was open for 40% -> 44% of each run, Pallas kernels for 0% -> 0%
where the time goes in v1:
time: 676 us; the launch traced here: 668 us
  waiting for transfers between devices  285 us (42%)
  local copies, waits for them, and re-layouts  146 us (22%)
  matrix products  144 us (21%)
  other arithmetic  72.3 us (11%)
  between operations  14.7 us (2%)
    reduce_scatter x1, waiting for transfers between devices, on_device(): lax.psum_scatter(jnp.concatenate([qkv_part, out_part], axis=1).astype(jnp...  207 us
    unnamed x53, local copies, waits for them, and re-layouts  70.1 us
    another operation x4, local copies, waits for them, and re-layouts, qkv_keep_table(): return jnp.stack(tables, axis=1)  48 us
    reduce_scatter x1, waiting for transfers between devices, on_device(): lax.psum_scatter(jnp.einsum('tc,mc->tm', row_piece, qkv_used, preferred_e...  42.7 us
    mul x1, other arithmetic, on_device(): qkv_used = qkv_weight.reshape(model_width, 3 * features) * qkv_keep  28.6 us
    dot_general x1, matrix products, on_device(): jnp.einsum('tm,tc->mc', gathered, grad_proj, preferred_element_type=jnp.f...  25.9 us
    concatenate x1, other arithmetic, on_device(): jnp.concatenate([qkv_part, out_part], axis=1).astype(jnp.bfloat16)  23.5 us
    broadcast_in_dim x5, local copies, waits for them, and re-layouts, expand_blocks(): jnp.broadcast_to(blocks.astype(jnp.bfloat16)[:, None, :, None], (row_bloc...  22.3 us
  transfers between devices with their start and end apart: 9, of which 5 were waited for; matrix products, arithmetic and copies ran while one was open for 44% of the time, Pallas kernels for 0%

profile of v1, /device:TPU:0, one launch (start us, length us, event | category | flops | bytes accessed | tf_op | source)
XLA Modules:
  0.0 668.4 jit_solution(1887015115992455011)
XLA Ops:
  7.9 3.1 collective-permute-start
  11.0 33.6 %copy.45 = bf16[4096,3,1024]{0,2,1:T(8,128)(2,1)} copy(bf16[4096,3,1024]{2,0,1:T(8,128)(2,1)} %param.15) | data formatting | bytes 50331648 | tf_op args[3]
  44.7 4.4 broadcast_in_dim.22
  49.1 13.3 %stack_reshape.9 = bf16[4096,1,1024]{0,2,1:T(8,128)(2,1)} reshape(bf16[32,128,8,128]{1,0,3,2:T(8,128)(2,1)} %broadcast_in_dim.22) | data formatting | bytes 16777216 | tf_op jit(solution)/shard_map/stack;reshape | solution.py:48
  62.4 4.4 broadcast_in_dim.25
  66.8 13.3 %stack_reshape.10 = bf16[4096,1,1024]{0,2,1:T(8,128)(2,1)} reshape(bf16[32,128,8,128]{1,0,3,2:T(8,128)(2,1)} %broadcast_in_dim.25) | data formatting | bytes 16777216 | tf_op jit(solution)/shard_map/stack;reshape | solution.py:48
  80.1 4.4 broadcast_in_dim.26
  84.5 13.3 %stack_reshape.11 = bf16[4096,1,1024]{0,2,1:T(8,128)(2,1)} reshape(bf16[32,128,8,128]{1,0,3,2:T(8,128)(2,1)} %broadcast_in_dim.26) | data formatting | bytes 16777216 | tf_op jit(solution)/shard_map/stack;reshape | solution.py:48
  97.8 1.3 collective-permute-start.1
  99.1 7.7 %constant_dynamic-update-slice_fusion.2 = bf16[4096,3,1024]{0,2,1:T(8,128)(2,1)} fusion(bf16[4096,1,1024]{0,2,1:T(8,128)(2,1)} %stack_reshape.9), kind=kLoop, calls=%fused_computation.52 | loop fusion | bytes 16777216
  106.8 7.8 %constant_dynamic-update-slice_fusion.1 = bf16[4096,3,1024]{0,2,1:T(8,128)(2,1)} fusion(bf16[4096,3,1024]{0,2,1:T(8,128)(2,1)} %constant_dynamic-update-slice_fusion.2, bf16[4096,1,1024]{0,2,1:T(8,128)(2,1)} %stack_reshape.10), kind=kLoop, calls=%fused_computation.51 | loop fusion | bytes 16777216
  114.6 12.2 %collective-permute-done.1 = bf16[128,4096]{1,0:T(8,128)(2,1)S(1)} collective-permute-done((bf16[128,4096]{1,0:T(8,128)(2,1)S(1)}, bf16[128,4096]{1,0:T(8,128)(2,1)S(1)}, u32[]{:S(2)}, u32[]{:S(2)}) %collective-permute-start.1) | collective-permute-done | bytes 1048608 | tf_op jit(solution)/shard_map/ppermute | solution.py:101
  126.9 8.0 %constant_dynamic-update-slice_fusion = bf16[4096,3,1024]{0,2,1:T(8,128)(2,1)} fusion(bf16[4096,3,1024]{0,2,1:T(8,128)(2,1)} %constant_dynamic-update-slice_fusion.1, bf16[4096,1,1024]{0,2,1:T(8,128)(2,1)} %stack_reshape.11), kind=kLoop, calls=%fused_computation.50 | loop fusion | bytes 16777216 | tf_op jit(solution)/shard_map/stack | solution.py:48
  135.0 28.6 %mul.85 = bf16[4096,3,1024]{0,2,1:T(8,128)(2,1)} multiply(bf16[4096,3,1024]{0,2,1:T(8,128)(2,1)} %copy.45, bf16[4096,3,1024]{0,2,1:T(8,128)(2,1)} %constant_dynamic-update-slice_fusion) | non-fusion elementwise | flops 12582912 | bytes 75497472 | tf_op jit(solution)/shard_map/mul | solution.py:65
  163.8 1.2 constant_dynamic-update-slice_fusion.10
  165.1 18.2 %convolution_convert_fusion.2 = bf16[3072,512]{1,0:T(8,128)(2,1)S(1)} fusion(bf16[4096,3072]{0,1:T(8,128)(2,1)} %bitcast.142, bf16[512,4096]{1,0:T(8,128)(2,1)} %all-gather.6.cloned.1.call-done), kind=kOutput, calls=%fused_computation.13 | convolution fusion | flops 12886474752 | bytes 32505856 | tf_op jit(solution)/shard_map/dot_general | solution.py:68
  183.3 1.5 convolution_convert_fusion.3
  184.9 2.5 constant_dynamic-update-slice_fusion.9
  187.3 2.4 constant_dynamic-update-slice_fusion.8
  189.7 1.1 constant_dynamic-update-slice_fusion.7
  190.8 1.1 constant_dynamic-update-slice_fusion.6
  191.9 1.0 constant_dynamic-update-slice_fusion.5
  192.9 1.1 constant_dynamic-update-slice_fusion.4
  194.0 1.1 constant_dynamic-update-slice_fusion.3
  195.0 1.4 select_convert_fusion.1
  196.5 2.0 copy-done.3
  198.4 2.8 fusion.14
  201.2 12.9 %all-gather.8.cloned.1.call-done = bf16[64,128,128]{2,1,0:T(8,128)(2,1)} async-done(((bf16[8,128,128]{2,1,0:T(8,128)(2,1)}), bf16[64,128,128]{2,1,0:T(8,128)(2,1)}) %all-gather.8.cloned.1.call-update) | async-done | bytes 2097168 | tf_op jit(solution)/shard_map/all_gather | solution.py:13
  214.3 4.4 fusion.7
  218.7 1.1 broadcast_in_dim.30
  219.9 15.7 %multiply_reduce_fusion = (f32[512,8]{0,1:T(8,128)S(1)}, f32[512,1024]{0,1:T(8,128)}) fusion(f32[8,128,512]{2,1,0:T(8,128)} %get-tuple-element.125, f32[512,8]{0,1:T(8,128)S(1)} %add_rsqrt_fusion, bf16[1024,4096]{1,0:T(8,128)(2,1)} %param.17, bf16[128,8,32,128]{3,2,1,0:T(8,128)(2,1)S(1)} %bitcast.139, ...), kind=kOutput, calls=%fused_computation.29 | convolution fusion | flops 4300730368 | bytes 25198596 | tf_op jit(solution)/shard_map/tm,fm->tf/dot_general | solution.py:105
  235.6 3.9 subtract_multiply_fusion
  239.5 3.1 convolution_convert_fusion.4
  243.1 13.3 %convolution_convert_fusion.1 = bf16[512,4096]{1,0:T(8,128)(2,1)} fusion(bf16[512,1024]{0,1:T(8,128)(2,1)} %bitcast.154, bf16[1024,4096]{1,0:T(8,128)(2,1)} %param.17, bf16[128,8,32,128]{3,2,1,0:T(8,128)(2,1)} %bitcast.140), kind=kOutput, calls=%fused_computation.12 | convolution fusion | flops 4301258752 | bytes 22020096 | tf_op jit(solution)/shard_map/dot_general | solution.py:93
  256.5 2.8 select_convert_fusion
  259.3 1.5 fusion.24
  260.7 2.9 fusion.10
  263.6 2.1 fusion.19
  266.6 2.0 fusion.15
  268.6 9.6 %all-gather.10.cloned.1.call-done = bf16[64,128,128]{2,1,0:T(8,128)(2,1)} async-done(((bf16[8,128,128]{2,1,0:T(8,128)(2,1)}), bf16[64,128,128]{2,1,0:T(8,128)(2,1)}) %all-gather.10.cloned.1.call-update) | async-done | bytes 2097168 | tf_op jit(solution)/shard_map/all_gather | solution.py:26
  278.3 8.0 %while.23 = (s32[]{:T(128)}, f32[8,128,128]{2,1,0:T(8,128)S(1)}, s32[]{:T(128)}, bf16[8,8,128,128]{3,2,1,0:T(8,128)(2,1)}, s32[]{:T(128)}, /*index=5*/s32[]{:T(128)}, s32[]{:T(128)}, s32[]{:T(128)}) while((s32[]{:T(128)}, f32[8,128,128]{2,1,0:T(8,128)S(1)}, s32[]{:T(128)}, bf16[8,8,128,128]{3,2,1,0:T(8,128)(2,1)}, s32[]{:T(128)}, ...), condition=%wide.region_6.7_spmd, body=%wide.region_5.6_spmd.sunk | while | flops 262150 | bytes 1310863 | solution.py:35
  278.3 1.2 convert_add_fusion.5
  279.5 1.1 convert_add_fusion.5
  280.6 1.1 convert_add_fusion.5
  281.7 1.1 convert_add_fusion.5
  282.8 1.1 convert_add_fusion.5
  283.9 1.1 convert_add_fusion.5
  285.0 1.1 convert_add_fusion.5
  286.2 3.6 fusion.9
  289.9 2.3 fusion.11
  292.5 19.6 %convolution_convert_fusion = bf16[512,4096]{1,0:T(8,128)(2,1)} fusion(bf16[512,3072]{0,1:T(8,128)(2,1)S(1)} %bitcast.156, bf16[4096,3072]{0,1:T(8,128)(2,1)} %bitcast.143), kind=kOutput, calls=%fused_computation.11 | convolution fusion | flops 12886999040 | bytes 32505856 | tf_op jit(solution)/shard_map/tc,mc->tm/dot_general | solution.py:138
  312.4 8.0 %broadcast_in_dim.58 = f32[32,128,8,128]{1,0,3,2:T(8,128)} broadcast(f32[32,8]{0,1:T(8,128)S(1)} %get-tuple-element.113), dimensions={0,2} | broadcast | bytes 16778240 | tf_op jit(solution)/shard_map/broadcast_in_dim | solution.py:40
  320.4 21.1 %fusion.1 = bf16[4096,1024]{0,1:T(8,128)(2,1)} fusion(f32[128,8,32,128]{3,2,1,0:T(8,128)} %bitcast.137, bf16[512,1024]{0,1:T(8,128)(2,1)S(1)} %bitcast.155, bf16[1024,4096]{1,0:T(8,128)(2,1)} %constant_dynamic-update-slice_fusion.3, s32[]{:T(128)S(6)} %select_n.33), kind=kOutput, calls=%fused_computation.6 | convolution fusion | flops 4303355904 | bytes 30408708 | tf_op jit(solution)/shard_map/tm,tf->mf/dot_general | solution.py:151
  341.5 25.9 %fusion = bf16[4096,3072]{0,1:T(8,128)(2,1)} fusion(bf16[4096,3072]{0,1:T(8,128)(2,1)} %bitcast.138, bf16[512,3072]{0,1:T(8,128)(2,1)S(1)} %bitcast.157, bf16[512,4096]{1,0:T(8,128)(2,1)} %all-gather.6.cloned.1.call-done), kind=kOutput, calls=%fused_computation.3 | convolution fusion | flops 12922650624 | bytes 57671680 | tf_op jit(solution)/shard_map/tm,tc->mc/dot_general | solution.py:149
  367.4 23.5 %pad_maximum_fusion = bf16[4096,4096]{0,1:T(8,128)(2,1)} fusion(bf16[4096,1024]{0,1:T(8,128)(2,1)} %fusion.1, bf16[4096,3072]{0,1:T(8,128)(2,1)} %fusion), kind=kLoop, calls=%fused_computation.4 | loop fusion | flops 67108864 | bytes 67108864 | tf_op jit(solution)/shard_map/concatenate | solution.py:154
  391.0 1.1 copy-done.9
  392.1 2.4 add_convert_fusion.2
  394.6 42.7 %reduce-scatter.6.cloned.1.call-done = bf16[128,4096]{1,0:T(8,128)(2,1)} async-done(((bf16[512,4096]{1,0:T(8,128)(2,1)}), bf16[128,4096]{1,0:T(8,128)(2,1)}) %reduce-scatter.6.cloned.1.call-update) | async-done | bytes 1048592 | tf_op jit(solution)/shard_map/reduce_scatter | solution.py:137
  437.3 2.4 add_convert_fusion
  439.7 206.8 %reduce-scatter.8.cloned.1.call-done = bf16[512,4096]{0,1:T(8,128)(2,1)} async-done(((bf16[4096,4096]{0,1:T(8,128)(2,1)}), bf16[512,4096]{0,1:T(8,128)(2,1)}) %reduce-scatter.8.cloned.1.call-update) | async-done | bytes 4194320 | tf_op jit(solution)/shard_map/reduce_scatter | solution.py:153
  646.5 3.4 convert_multiply_fusion.1
  649.9 3.3 slice.41
  653.2 1.5 slice_bitcast_fusion
  654.7 6.6 copy.59
  (68 shorter events, 3.6 us)
Async XLA Ops:
  7.2 157.8 %all-gather.6.cloned.1.call-start = ((), (), s32[]{:S(2)}) async-start(), calls=%async_computation.3 | async-start | bytes 5242880 | tf_op jit(solution)/shard_map/all_gather | solution.py:67
  7.9 206.2 %all-gather.8.cloned.1.call-start = ((), (), s32[]{:S(2)}) async-start(), calls=%async_computation.7 | async-start | bytes 2359296 | tf_op jit(solution)/shard_map/all_gather | solution.py:13
  7.9 89.8 %collective-permute-start = (bf16[128,4096]{1,0:T(8,128)(2,1)}, bf16[128,4096]{1,0:T(8,128)(2,1)S(1)}, u32[]{:S(2)}, u32[]{:S(2)}) collective-permute-start(bf16[128,4096]{1,0:T(8,128)(2,1)} %param.19), channel_id=1, source_target_pairs={{0,1},{1,2},{2,3},{3,0},{4,5},{5,6},{6,7},{7,4},{8,9},{9,10},{10,1... | collective-permute-start | bytes 3145736 | tf_op jit(solution)/shard_map/ppermute | solution.py:101
  11.0 33.6 %copy-start.19 = (s32[3,32,8]{1,2,0:T(8,128)S(1)}, s32[3,32,8]{1,2,0:T(8,128)}, u32[]{:S(2)}) copy-start(s32[3,32,8]{1,2,0:T(8,128)} %param.16) | copy-start | bytes 9220
  97.8 9.1 %copy-start.10 = (bf16[128,4096]{1,0:T(8,128)(2,1)}, bf16[128,4096]{1,0:T(8,128)(2,1)S(1)}, u32[]{:S(2)}) copy-start(bf16[128,4096]{1,0:T(8,128)(2,1)S(1)} %collective-permute-done) | copy-start | bytes 3145732
  97.8 29.0 %collective-permute-start.1 = (bf16[128,4096]{1,0:T(8,128)(2,1)S(1)}, bf16[128,4096]{1,0:T(8,128)(2,1)S(1)}, u32[]{:S(2)}, u32[]{:S(2)}) collective-permute-start(bf16[128,4096]{1,0:T(8,128)(2,1)S(1)} %collective-permute-done), channel_id=1, source_target_pairs={{0,1},{1,2},{2,3},{3,0},{4,5},{5,6},{6,7},{7,4},{8,9},{9,10},{10,1... | collective-permute-start | bytes 3145736 | tf_op jit(solution)/shard_map/ppermute | solution.py:101
  126.8 8.2 %copy-start.12 = (bf16[128,4096]{1,0:T(8,128)(2,1)}, bf16[128,4096]{1,0:T(8,128)(2,1)S(1)}, u32[]{:S(2)}) copy-start(bf16[128,4096]{1,0:T(8,128)(2,1)S(1)} %collective-permute-done.1) | copy-start | bytes 3145732
  126.8 37.0 %collective-permute-start.2 = (bf16[128,4096]{1,0:T(8,128)(2,1)S(1)}, bf16[128,4096]{1,0:T(8,128)(2,1)S(1)}, u32[]{:S(2)}, u32[]{:S(2)}) collective-permute-start(bf16[128,4096]{1,0:T(8,128)(2,1)S(1)} %collective-permute-done.1), channel_id=1, source_target_pairs={{0,1},{1,2},{2,3},{3,0},{4,5},{5,6},{6,7},{7,4},{8,9},{9,10},{10,1... | collective-permute-start | bytes 3145736 | tf_op jit(solution)/shard_map/ppermute | solution.py:101
  135.0 28.7 %copy-start.20 = (s32[8,32]{1,0:T(8,128)S(1)}, s32[8,32]{1,0:T(8,128)}, u32[]{:S(2)}) copy-start(s32[8,32]{1,0:T(8,128)} %param.18) | copy-start | bytes 3076
  135.0 28.7 %copy-start.17 = (s32[512,8]{0,1:T(8,128)S(1)}, s32[512,8]{0,1:T(8,128)}, u32[]{:S(2)}) copy-start(s32[512,8]{0,1:T(8,128)} %param.13) | copy-start | bytes 49156
  135.0 28.7 %copy-start.18 = (s32[512,8]{0,1:T(8,128)S(1)}, s32[512,8]{0,1:T(8,128)}, u32[]{:S(2)}) copy-start(s32[512,8]{0,1:T(8,128)} %param.14) | copy-start | bytes 49156
  163.8 1.3 copy-start.14
  183.3 13.2 %copy-start.1 = (bf16[3072,512]{1,0:T(8,128)(2,1)}, bf16[3072,512]{1,0:T(8,128)(2,1)S(1)}, u32[]{:S(2)}) copy-start(bf16[3072,512]{1,0:T(8,128)(2,1)S(1)} %convolution_convert_fusion.2) | copy-start | bytes 9437188
  184.8 93.4 %all-gather.10.cloned.1.call-start = ((), (), s32[]{:S(2)}) async-start(), calls=%async_computation.8 | async-start | bytes 2359296 | tf_op jit(solution)/shard_map/all_gather | solution.py:26
  184.8 4.9 copy-start.5
  184.8 6.0 copy-start.15
  184.8 7.0 %copy-start.13 = (bf16[128,4096]{1,0:T(8,128)(2,1)S(1)}, bf16[128,4096]{1,0:T(8,128)(2,1)}, u32[]{:S(2)}) copy-start(bf16[128,4096]{1,0:T(8,128)(2,1)} %copy-done.12) | copy-start | bytes 3145732
  187.3 5.6 copy-start.11
  196.5 2.0 copy-start.3
  219.9 15.7 %copy-start = (bf16[8,128,32,128]{3,2,1,0:T(8,128)(2,1)}, bf16[8,128,32,128]{3,2,1,0:T(8,128)(2,1)S(1)}, u32[]{:S(2)}) copy-start(bf16[8,128,32,128]{3,2,1,0:T(8,128)(2,1)S(1)} %broadcast_in_dim.30) | copy-start | bytes 25165828
  242.6 148.4 %reduce-scatter.4.cloned.1.call-start = ((), (), s32[]{:S(2)}) async-start(), calls=%async_computation.4 | async-start | bytes 5242880 | tf_op jit(solution)/shard_map/reduce_scatter | solution.py:92
  256.4 180.9 %reduce-scatter.6.cloned.1.call-start = ((), (), s32[]{:S(2)}) async-start(), calls=%async_computation.5 | async-start | bytes 5242880 | tf_op jit(solution)/shard_map/reduce_scatter | solution.py:137
  256.5 2.8 copy-start.2
  263.6 2.9 copy-start.4
  278.3 11.6 %copy-start.7 = (f32[8,128,512]{2,1,0:T(8,128)S(1)}, f32[8,128,512]{2,1,0:T(8,128)}, u32[]{:S(2)}) copy-start(f32[8,128,512]{2,1,0:T(8,128)} %fusion.19) | copy-start | bytes 6291460
  286.2 5.9 copy-start.16
  312.1 334.3 %reduce-scatter.8.cloned.1.call-start = ((), (), s32[]{:S(2)}) async-start(), calls=%async_computation.6 | async-start | bytes 37748736 | tf_op jit(solution)/shard_map/reduce_scatter | solution.py:153
  312.4 8.0 %copy-start.8 = (bf16[512,8,128]{0,2,1:T(8,128)(2,1)S(1)}, bf16[512,8,128]{0,2,1:T(8,128)(2,1)}, u32[]{:S(2)}) copy-start(bf16[512,8,128]{0,2,1:T(8,128)(2,1)} %get-tuple-element.120) | copy-start | bytes 3145732
  390.9 1.2 copy-start.9
  390.9 46.4 %copy-start.6 = (bf16[128,4096]{1,0:T(8,128)(2,1)S(1)}, bf16[128,4096]{1,0:T(8,128)(2,1)}, u32[]{:S(2)}) copy-start(bf16[128,4096]{1,0:T(8,128)(2,1)} %param.19) | copy-start | bytes 3145732
Sparse Core Ops, SparseCore 0:
  9.6 97.1 all-gather.5
  184.9 29.1 all-gather.7
  242.7 35.4 all-gather.9
  280.9 76.7 reduce-scatter.3
  360.0 77.2 reduce-scatter.5
  440.7 205.7 reduce-scatter.7
